TPU v7x, 128 devices: a whole 4x4x4 slice. The times are simulated.
128 devices in a mesh: dp: 8 (over x, core), fsdp: 16 (over y, z).
Axes of the slice: x: 4, y: 4, z: 4, core: 2. Of those that a mesh axis runs over, the one named last changes fastest.
Arguments:
- tokens: bfloat16 [65536, 8192], P(('dp', 'fsdp')), may hold values from -6 to 6
- frozen_value_matrix: bfloat16 [8192, 1024], P('fsdp'), may hold values from -0.0625 to 0.0625
- adapter_down_maps: bfloat16 [512, 64, 8192], P('dp', None, 'fsdp'), may hold values from -0.0625 to 0.0625
- adapter_up_maps: bfloat16 [512, 64, 1024], P('dp', None, 'fsdp'), may hold values from -0.375 to 0.375
- value_output_gradient: bfloat16 [65536, 1024], P(('dp', 'fsdp')), may hold values from -0.125 to 0.125
- window_composer_position: int32 [8, 64], P('dp'), may hold values from 0 to 3
- needed_composers: int32 [8, 4], replicated, may hold values from 0 to 511, as said below
- composer_storage_index: int32 [512], replicated, may hold values from 0 to 511, as said below
Outputs:
- value: bfloat16 [65536, 1024], P(('dp', 'fsdp'))
- grad_down: float32 [512, 64, 8192], P('dp', None, 'fsdp')
- grad_up: float32 [512, 64, 1024], P('dp', None, 'fsdp')
Inputs may be any that keep to these rules, and one draw needn't show every extreme that they name: Every storage index appears once: the adapters and gradients of composer c lie at index composer_storage_index[c]; composer c is owned by index composer_storage_index[c] // 64 of dp. `needed_composers`: the 4 composers of one row have 4 different owners along dp.
All inputs are finite; a program needn't handle non-finite values.
Results may differ from a plain program's by a relative error of at most 0.004.
Values may be sent and summed in bfloat16 or wider, within the bound.
No kernel may reach another device: no remote copies, remote signals or barrier semaphores. Data moves between devices by JAX's collectives and lax.ppermute only.
A program may use at most 128 MiB of HBM per device.

v0:
```python
import jax
import jax.numpy as jnp
from jax import lax
from jax.sharding import PartitionSpec as P

WIN = 128
ADAPTER_SCALE = 2.0


def body(
    tokens,
    frozen_value_matrix,
    adapter_down_maps,
    adapter_up_maps,
    value_output_gradient,
    window_composer_position,
    needed_composers,
    composer_storage_index,
):
    f32, bf16 = (jnp.float32, jnp.bfloat16)
    dp_count = lax.axis_size("dp")
    fsdp_count = lax.axis_size("fsdp")
    group_index = lax.axis_index("dp")
    member_index = lax.axis_index("fsdp")
    tok_rows, width = tokens.shape
    value_cols = frozen_value_matrix.shape[1]
    rank = adapter_down_maps.shape[1]
    each_owner_rows = adapter_down_maps.shape[0]
    down_cols = adapter_down_maps.shape[2]
    up_cols = adapter_up_maps.shape[2]
    list_len = needed_composers.shape[1]
    windows = tok_rows // WIN
    part_cols = value_cols // dp_count
    w_part = lax.dynamic_slice_in_dim(
        frozen_value_matrix, group_index * part_cols, part_cols, axis=1
    )
    w_part_full = lax.all_gather(w_part, "fsdp", axis=0, tiled=True)
    up_x = [(i, (i + 2) % dp_count) for i in range(dp_count)]
    down_x = [(i, (i - 2) % dp_count) for i in range(dp_count)]
    from_left = lax.ppermute(w_part_full, "dp", up_x)
    from_right = lax.ppermute(w_part_full, "dp", down_x)
    half_part = part_cols // 2
    far_a = lax.ppermute(from_left[:, :half_part], "dp", up_x)
    far_b = lax.ppermute(from_right[:, half_part:], "dp", down_x)
    far = jnp.concatenate([far_a, far_b], axis=1)
    same_parity = [w_part_full, from_left, far, from_right]
    w_own = jnp.concatenate(same_parity, axis=1)
    w_partner = lax.ppermute(w_own, "dp", [(i, i ^ 1) for i in range(dp_count)])
    out_own = jnp.dot(tokens, w_own, preferred_element_type=f32)
    out_partner = jnp.dot(tokens, w_partner, preferred_element_type=f32)
    held = jnp.concatenate([out_own, out_partner], axis=1).reshape(tok_rows, dp_count, part_cols)
    part_ids = jnp.arange(dp_count, dtype=jnp.int32)
    partner_index = group_index ^ 1
    same = part_ids % 2 == group_index % 2
    where_held = jnp.where(
        same,
        (group_index - part_ids) % dp_count // 2,
        dp_count // 2 + (partner_index - part_ids) % dp_count // 2,
    )
    frozen_rows = jnp.take(held, where_held, axis=1).reshape(tok_rows, value_cols)
    list_slot = jnp.take(composer_storage_index, needed_composers, axis=0)
    list_owner = list_slot // each_owner_rows
    list_local = list_slot % each_owner_rows
    owned_here = list_owner == group_index
    locally_owned_slots = jnp.sum(jnp.where(owned_here, list_local, 0), axis=1)
    owned_any = jnp.any(owned_here, axis=1)
    send = jnp.concatenate(
        [
            jnp.take(adapter_down_maps, locally_owned_slots, axis=0),
            jnp.take(adapter_up_maps, locally_owned_slots, axis=0),
        ],
        axis=2,
    )
    send = jnp.where(owned_any[:, None, None], send, jnp.zeros((), send.dtype))
    got = lax.all_to_all(send, "dp", split_axis=0, concat_axis=0, tiled=True)
    my_owner = lax.dynamic_index_in_dim(list_owner, group_index, 0, keepdims=False)
    slab = jnp.take(got, my_owner, axis=0)
    shares = lax.all_gather(slab, "fsdp", axis=0, tiled=False)
    full_down = shares[..., :down_cols].transpose(1, 2, 0, 3).reshape(list_len, rank, width)
    full_up = shares[..., down_cols:].transpose(1, 2, 0, 3).reshape(list_len, rank, value_cols)
    group_picks = window_composer_position[0]
    my_picks = lax.dynamic_slice_in_dim(group_picks, member_index * windows, windows, 0)
    slot_range = jnp.arange(list_len, dtype=jnp.int32)
    token_hot = jnp.broadcast_to(
        my_picks[:, None, None] == slot_range[None, None, :], (windows, WIN, list_len)
    ).reshape(tok_rows, list_len)
    hot_f = token_hot.astype(f32)
    down_flat = full_down.reshape(list_len * rank, width)
    up_flat = full_up.reshape(list_len * rank, value_cols)
    low_all = lax.dot_general(
        tokens, down_flat, (((1,), (1,)), ((), ())), preferred_element_type=f32
    ).reshape(tok_rows, list_len, rank)
    low = jnp.sum(low_all * hot_f[:, :, None], axis=1).astype(bf16)
    hot_h = token_hot.astype(bf16)
    masked_low = (hot_h[:, :, None] * low[:, None, :]).reshape(tok_rows, list_len * rank)
    adapter_change = jnp.dot(masked_low, up_flat, preferred_element_type=f32)
    value = (frozen_rows + ADAPTER_SCALE * adapter_change).astype(bf16)
    back_all = lax.dot_general(
        value_output_gradient, up_flat, (((1,), (1,)), ((), ())), preferred_element_type=f32
    ).reshape(tok_rows, list_len, rank)
    back = (ADAPTER_SCALE * jnp.sum(back_all * hot_f[:, :, None], axis=1)).astype(bf16)
    masked_back = (hot_h[:, :, None] * back[:, None, :]).reshape(tok_rows, list_len * rank)
    scaled_masked_low = masked_low * jnp.asarray(ADAPTER_SCALE, bf16)
    contract = (((0,), (0,)), ((), ()))
    part_down = lax.dot_general(masked_back, tokens, contract, preferred_element_type=f32)
    part_up = lax.dot_general(
        scaled_masked_low, value_output_gradient, contract, preferred_element_type=f32
    )
    rows = list_len * rank
    up_rows = rows * up_cols // down_cols
    up_as_rows = (
        part_up.reshape(rows, fsdp_count, up_cols)
        .transpose(1, 0, 2)
        .reshape(fsdp_count, up_rows, down_cols)
        .transpose(1, 0, 2)
        .reshape(up_rows, fsdp_count * down_cols)
    )
    both = jnp.concatenate([part_down, up_as_rows], axis=0)
    summed = lax.psum_scatter(both, "fsdp", scatter_dimension=1, tiled=True)
    per_slot = jnp.concatenate(
        [
            summed[:rows].reshape(list_len, rank, down_cols),
            summed[rows:].reshape(list_len, up_rows // list_len, down_cols),
        ],
        axis=1,
    )
    owner_range = jnp.arange(dp_count, dtype=jnp.int32)
    to_owner = my_owner[None, :] == owner_range[:, None]
    pick_index = jnp.sum(jnp.where(to_owner, slot_range[None, :], 0), axis=1)
    owner_has = jnp.any(to_owner, axis=1)
    send_grad = jnp.take(per_slot, pick_index, axis=0)
    send_grad = jnp.where(owner_has[:, None, None], send_grad, 0.0)
    back_grad = lax.all_to_all(send_grad, "dp", split_axis=0, concat_axis=0, tiled=True)
    land = jnp.where(owned_any, locally_owned_slots, 0)
    arrived = jnp.where(owned_any[:, None, None], back_grad, 0.0)
    grad_down = jnp.zeros((each_owner_rows, rank, down_cols), f32).at[land].add(arrived[:, :rank])
    grad_up = (
        jnp.zeros((each_owner_rows, rank, up_cols), f32)
        .at[land]
        .add(arrived[:, rank:].reshape(dp_count, rank, up_cols))
    )
    return (value, grad_down, grad_up)


def solution(mesh):
    return jax.shard_map(
        body,
        mesh=mesh,
        in_specs=(
            P(("dp", "fsdp"), None),
            P("fsdp", None),
            P("dp", None, "fsdp"),
            P("dp", None, "fsdp"),
            P(("dp", "fsdp"), None),
            P("dp", None),
            P(),
            P(),
        ),
        out_specs=(P(("dp", "fsdp"), None), P("dp", None, "fsdp"), P("dp", None, "fsdp")),
        check_vma=False,
    )
```

profile of v0, /device:TPU:1, one launch (start us, length us, event | category | flops | bytes accessed | tf_op | source)
XLA Modules:
  0.0 275.7 jit_solution(16079173203989045500)
XLA Ops:
  11.8 2.8 %gather_fusion.2 = bf16[8,64,512]{2,1,0:T(8,128)(2,1)S(1)} fusion(bf16[64,64,512]{2,1,0:T(8,128)(2,1)} %param.10, s32[1024]{0:T(1024)S(1)} %pad_clamp_fusion.2), kind=kCustom, calls=%fused_computation.2 | custom fusion | bytes 1048608 | tf_op jit(solution)/shard_map/jit(_take)/gather | solution.py:69
  15.9 5.8 %all-to-all-start = ((bf16[8,64,576]{2,1,0:T(8,128)(2,1)}), bf16[8,64,576]{2,1,0:T(8,128)(2,1)S(1)}, u32[]{:S(2)}, u32[]{:S(2)}) async-start(bf16[8,64,576]{2,1,0:T(8,128)(2,1)} %maximum_select_fusion), calls=%async_computation | async-start | bytes 1310720 | tf_op jit(solution)/shard_map/all_to_all | solution.py:75
  21.7 10.9 %all-to-all-done = bf16[8,64,576]{2,1,0:T(8,128)(2,1)S(1)} async-done(((bf16[8,64,576]{2,1,0:T(8,128)(2,1)}), bf16[8,64,576]{2,1,0:T(8,128)(2,1)S(1)}, u32[]{:S(2)}, u32[]{:S(2)}) %all-to-all-start) | async-done | bytes 589856 | tf_op jit(solution)/shard_map/all_to_all | solution.py:75
  35.8 55.6 %all-gather.5.cloned.1.call-done = bf16[16,4,64,576]{3,2,1,0:T(8,128)(2,1)} async-done(((bf16[1,4,64,576]{3,2,1,0:T(8,128)(2,1)}), bf16[16,4,64,576]{3,2,1,0:T(8,128)(2,1)}) %all-gather.5.cloned.1.call-update) | async-done | bytes 4718608 | tf_op jit(solution)/shard_map/all_gather | solution.py:78
  94.4 2.1 reshape_reshape.7
  96.5 2.9 %slice_bitcast_fusion = bf16[4,64,16,512]{3,1,0,2:T(8,128)(2,1)S(1)} fusion(bf16[16,4,64,576]{3,2,1,0:T(8,128)(2,1)} %all-gather.5.cloned.1.call-done), kind=kLoop, calls=%fused_computation.9 | loop fusion | bytes 8388608 | tf_op jit(solution)/shard_map/transpose | solution.py:79
  99.9 2.4 copy.32
  102.3 4.4 %copy.44 = bf16[32,8,16,512]{3,1,2,0:T(8,128)(2,1)S(1)} copy(bf16[32,8,16,512]{3,2,1,0:T(8,128)(2,1)S(1)} %bitcast.101) | data formatting | bytes 8388608
  106.7 2.4 fusion.20
  113.9 9.4 %fusion.22 = f32[256,8192]{1,0:T(8,128)} fusion(bf16[512,256]{0,1:T(8,128)(2,1)S(1)} %bitcast.112, bf16[512,8192]{1,0:T(8,128)(2,1)} %param.8), kind=kOutput, calls=%fused_computation.127 | convolution fusion | flops 2147483648 | bytes 17039360 | tf_op jit(solution)/shard_map/dot_general | solution.py:105
  123.3 8.2 %pad_maximum_fusion = f32[288,8192]{1,0:T(8,128)} fusion(f32[32,8192]{1,0:T(8,128)S(1)} %bitcast.107, f32[256,8192]{1,0:T(8,128)} %fusion.22), kind=kLoop, calls=%fused_computation.8 | loop fusion | flops 2359296 | bytes 18874368 | tf_op jit(solution)/shard_map/concatenate | solution.py:118
  131.5 9.2 %all-gather.3.cloned.1.call-done = bf16[8192,128]{0,1:T(8,128)(2,1)} async-done(((bf16[512,128]{0,1:T(8,128)(2,1)}), bf16[8192,128]{0,1:T(8,128)(2,1)}) %all-gather.3.cloned.1.call-update) | async-done | bytes 2097168 | tf_op jit(solution)/shard_map/all_gather | solution.py:37
  143.4 44.4 %collective-permute-done = bf16[8192,128]{0,1:T(8,128)(2,1)S(1)} collective-permute-done((bf16[8192,128]{0,1:T(8,128)(2,1)}, bf16[8192,128]{0,1:T(8,128)(2,1)S(1)}, u32[]{:S(2)}, u32[]{:S(2)}) %collective-permute-start) | collective-permute-done | bytes 2097184 | tf_op jit(solution)/shard_map/ppermute | solution.py:40
  188.0 3.2 %constant_dynamic-update-slice_fusion.4 = bf16[8192,512]{0,1:T(8,128)(2,1)} fusion(bf16[8192,128]{0,1:T(8,128)(2,1)} %all-gather.3.cloned.1.call-done), kind=kLoop, calls=%fused_computation.35 | loop fusion | bytes 4194304
  191.3 2.7 collective-permute-start.3
  195.5 16.0 %collective-permute-done.1 = bf16[8192,64]{0,1:T(8,128)(2,1)S(1)} collective-permute-done((bf16[8192,64]{0,1:T(8,128)(2,1)S(1)}, bf16[8192,64]{0,1:T(8,128)(2,1)S(1)}, u32[]{:S(2)}, u32[]{:S(2)}) %collective-permute-start.1) | collective-permute-done | bytes 1048608 | tf_op jit(solution)/shard_map/ppermute | solution.py:43
  216.5 3.4 %collective-permute-start.4 = (bf16[8192,512]{0,1:T(8,128)(2,1)}, bf16[8192,512]{0,1:T(8,128)(2,1)}, u32[]{:S(2)}, u32[]{:S(2)}) collective-permute-start(bf16[8192,512]{0,1:T(8,128)(2,1)} %constant_dynamic-update-slice_fusion), channel_id=1, source_target_pairs={{0,16},{16,0},{32,48},{48,32},{64,80},{80,64},{96,112},{112,96},{1... | collective-permute-start | bytes 25165832 | tf_op jit(solution)/shard_map/ppermute | solution.py:48
  220.2 11.5 %convolution_bitcast_fusion.2 = f32[512,512]{0,1:T(8,128)} fusion(bf16[8192,512]{0,1:T(8,128)(2,1)} %constant_dynamic-update-slice_fusion, bf16[512,8192]{1,0:T(8,128)(2,1)} %param.8), kind=kOutput, calls=%fused_computation.14 | convolution fusion | flops 4294967296 | bytes 17825792 | tf_op jit(solution)/shard_map/dot_general | solution.py:49
  235.6 5.1 %all-to-all-start.1 = ((f32[8,72,512]{2,1,0:T(8,128)}), f32[8,72,512]{2,1,0:T(8,128)}, u32[]{:S(2)}, u32[]{:S(2)}) async-start(f32[8,72,512]{2,1,0:T(8,128)} %select_select_fusion), calls=%async_computation.2 | async-start | bytes 2359296 | tf_op jit(solution)/shard_map/all_to_all | solution.py:133
  240.7 9.6 %convolution_bitcast_fusion.1 = f32[512,512]{0,1:T(8,128)S(1)} fusion(bf16[8192,512]{0,1:T(8,128)(2,1)} %collective-permute-done.4, bf16[512,8192]{1,0:T(8,128)(2,1)} %param.8), kind=kOutput, calls=%fused_computation.13 | convolution fusion | flops 4294967296 | bytes 17825792 | tf_op jit(solution)/shard_map/dot_general | solution.py:50
  250.5 2.0 gather_fusion
  252.5 1.9 copy.39
  259.0 4.5 %broadcast_in_dim.151 = f32[64,64,512]{2,1,0:T(8,128)} broadcast(f32[]{:T(128)} %constant.200.clone.1), dimensions={} | broadcast | bytes 8388612 | tf_op jit(solution)/shard_map/broadcast_in_dim | solution.py:136
  263.5 3.2 %scatter_fusion = f32[64,64,512]{2,1,0:T(8,128)} fusion(f32[64,64,512]{2,1,0:T(8,128)} %broadcast_in_dim.151, s32[8]{0:T(128)S(1)} %get-tuple-element.13, f32[8,64,512]{2,1,0:T(8,128)S(1)} %slice.50), kind=kCustom, calls=%fused_computation.6 | custom fusion | flops 262144 | bytes 3145760 | tf_op jit(solution)/shard_map/scatter-add | solution.py:136
  (103 shorter events, 37.9 us)
Async XLA Ops:
  7.2 26.9 %copy-start = (bf16[512,1024]{1,0:T(8,128)(2,1)S(1)}, bf16[512,1024]{1,0:T(8,128)(2,1)}, u32[]{:S(2)}) copy-start(bf16[512,1024]{1,0:T(8,128)(2,1)} %param.9) | copy-start | bytes 3145732
  9.5 25.5 %copy-start.8 = (s32[1,64]{1,0:T(1,128)S(1)}, s32[1,64]{1,0:T(1,128)}, u32[]{:S(2)}) copy-start(s32[1,64]{1,0:T(1,128)} %param.13) | copy-start | bytes 772
  9.5 25.7 %copy-start.4 = (bf16[512,1024]{1,0:T(8,128)(2,1)S(1)}, bf16[512,1024]{1,0:T(8,128)(2,1)}, u32[]{:S(2)}) copy-start(bf16[512,1024]{1,0:T(8,128)(2,1)} %param.12) | copy-start | bytes 3145732
  15.9 16.7 %all-to-all-start = ((bf16[8,64,576]{2,1,0:T(8,128)(2,1)}), bf16[8,64,576]{2,1,0:T(8,128)(2,1)S(1)}, u32[]{:S(2)}, u32[]{:S(2)}) async-start(bf16[8,64,576]{2,1,0:T(8,128)(2,1)} %maximum_select_fusion), calls=%async_computation | async-start | bytes 1310720 | tf_op jit(solution)/shard_map/all_to_all | solution.py:75
  21.7 69.7 %all-gather.5.cloned.1.call-start = ((), (), s32[]{:S(2)}) async-start(), calls=%async_computation.4 | async-start | bytes 5570560 | tf_op jit(solution)/shard_map/all_gather | solution.py:78
  34.0 106.7 %all-gather.3.cloned.1.call-start = ((), (), s32[]{:S(2)}) async-start(), calls=%async_computation.3 | async-start | bytes 2228224 | tf_op jit(solution)/shard_map/all_gather | solution.py:37
  35.0 196.7 %reduce-scatter.2.cloned.1.call-start = ((), (), s32[]{:S(2)}) async-start(), calls=%async_computation.5 | async-start | bytes 10027008 | tf_op jit(solution)/shard_map/reduce_scatter | solution.py:119
  96.5 3.4 %copy-start.2 = (bf16[256,1024]{1,0:T(8,128)(2,1)}, bf16[256,1024]{1,0:T(8,128)(2,1)S(1)}, u32[]{:S(2)}) copy-start(bf16[256,1024]{1,0:T(8,128)(2,1)S(1)} %reshape_reshape.7) | copy-start | bytes 1572868
  99.9 6.8 %slice-start = ((s8[8388608]{0:T(1024)(128)(4,1)}), s8[4194304]{0:T(1024)(128)(4,1)S(1)}, s32[]{:S(2)}) async-start(s8[8388608]{0:T(1024)(128)(4,1)} %bitcast.103), calls=%async_computation.6 | async-start | bytes 8388608
  102.3 4.4 %slice-start.1 = ((s8[8388608]{0:T(1024)(128)(4,1)}), s8[4194304]{0:T(1024)(128)(4,1)S(1)}, s32[]{:S(2)}) async-start(s8[8388608]{0:T(1024)(128)(4,1)} %bitcast.103), calls=%async_computation.7 | async-start | bytes 8388608
  140.7 47.1 %collective-permute-start = (bf16[8192,128]{0,1:T(8,128)(2,1)}, bf16[8192,128]{0,1:T(8,128)(2,1)S(1)}, u32[]{:S(2)}, u32[]{:S(2)}) collective-permute-start(bf16[8192,128]{0,1:T(8,128)(2,1)} %all-gather.3.cloned.1.call-done), channel_id=1, source_target_pairs={{0,32},{16,48},{32,64},{48,80},{64,96},{80,112},{96,0},{112,16},{1... | collective-permute-start | bytes 6291464 | tf_op jit(solution)/shard_map/ppermute | solution.py:40
  141.9 49.3 %collective-permute-start.2 = (bf16[8192,128]{0,1:T(8,128)(2,1)}, bf16[8192,128]{0,1:T(8,128)(2,1)S(1)}, u32[]{:S(2)}, u32[]{:S(2)}) collective-permute-start(bf16[8192,128]{0,1:T(8,128)(2,1)} %all-gather.3.cloned.1.call-done), channel_id=1, source_target_pairs={{0,96},{16,112},{32,0},{48,16},{64,32},{80,48},{96,64},{112,80},{1... | collective-permute-start | bytes 6291464 | tf_op jit(solution)/shard_map/ppermute | solution.py:41
  187.9 23.6 %collective-permute-start.1 = (bf16[8192,64]{0,1:T(8,128)(2,1)S(1)}, bf16[8192,64]{0,1:T(8,128)(2,1)S(1)}, u32[]{:S(2)}, u32[]{:S(2)}) collective-permute-start(bf16[8192,64]{0,1:T(8,128)(2,1)S(1)} %slice.44), channel_id=1, source_target_pairs={{0,32},{16,48},{32,64},{48,80},{64,96},{80,112},{96,0},{112,16},{1... | collective-permute-start | bytes 3145736 | tf_op jit(solution)/shard_map/ppermute | solution.py:43
  191.3 22.7 %collective-permute-start.3 = (bf16[8192,64]{0,1:T(8,128)(2,1)S(1)}, bf16[8192,64]{0,1:T(8,128)(2,1)S(1)}, u32[]{:S(2)}, u32[]{:S(2)}) collective-permute-start(bf16[8192,64]{0,1:T(8,128)(2,1)S(1)} %slice.45), channel_id=1, source_target_pairs={{0,96},{16,112},{32,0},{48,16},{64,32},{80,48},{96,64},{112,80},{1... | collective-permute-start | bytes 3145736 | tf_op jit(solution)/shard_map/ppermute | solution.py:44
  216.5 24.3 %collective-permute-start.4 = (bf16[8192,512]{0,1:T(8,128)(2,1)}, bf16[8192,512]{0,1:T(8,128)(2,1)}, u32[]{:S(2)}, u32[]{:S(2)}) collective-permute-start(bf16[8192,512]{0,1:T(8,128)(2,1)} %constant_dynamic-update-slice_fusion), channel_id=1, source_target_pairs={{0,16},{16,0},{32,48},{48,32},{64,80},{80,64},{96,112},{112,96},{1... | collective-permute-start | bytes 25165832 | tf_op jit(solution)/shard_map/ppermute | solution.py:48
  235.6 21.8 %all-to-all-start.1 = ((f32[8,72,512]{2,1,0:T(8,128)}), f32[8,72,512]{2,1,0:T(8,128)}, u32[]{:S(2)}, u32[]{:S(2)}) async-start(f32[8,72,512]{2,1,0:T(8,128)} %select_select_fusion), calls=%async_computation.2 | async-start | bytes 2359296 | tf_op jit(solution)/shard_map/all_to_all | solution.py:133
  240.7 9.6 %copy-start.7 = (f32[512,512]{0,1:T(8,128)S(1)}, f32[512,512]{0,1:T(8,128)}, u32[]{:S(2)}) copy-start(f32[512,512]{0,1:T(8,128)} %convolution_bitcast_fusion.2) | copy-start | bytes 3145732
  250.5 4.0 %copy-start.3 = (bf16[256,1024]{1,0:T(8,128)(2,1)S(1)}, bf16[256,1024]{1,0:T(8,128)(2,1)}, u32[]{:S(2)}) copy-start(bf16[256,1024]{1,0:T(8,128)(2,1)} %copy-done.2) | copy-start | bytes 1572868
  250.5 4.0 %copy-start.6 = (bf16[512,4,64]{0,2,1:T(8,128)(2,1)S(1)}, bf16[512,4,64]{0,2,1:T(8,128)(2,1)}, u32[]{:S(2)}) copy-start(bf16[512,4,64]{0,2,1:T(8,128)(2,1)} %get-tuple-element.11) | copy-start | bytes 786436
  259.0 10.2 %copy-start.1 = (bf16[512,1024]{1,0:T(8,128)(2,1)S(1)}, bf16[512,1024]{1,0:T(8,128)(2,1)}, u32[]{:S(2)}) copy-start(bf16[512,1024]{1,0:T(8,128)(2,1)} %param.9) | copy-start | bytes 3145732
  267.9 1.3 copy-start.5
Sparse Core Ops, SparseCore 0:
  34.2 57.1 all-gather.4
  94.1 46.5 all-gather.2
  144.2 86.6 reduce-scatter.1
where the time goes:
time: 276 us
  waiting for transfers between devices  139 us (50%)
  local copies, waits for them, and re-layouts  48.5 us (18%)
  matrix products  35.2 us (13%)
  starting transfers between devices  20 us (7%)
  other arithmetic  18.9 us (7%)
  between operations  14.2 us (5%)
    all_gather x1, waiting for transfers between devices, body(): shares = lax.all_gather(slab, 'fsdp', axis=0, tiled=False)  55.6 us
    ppermute x1, waiting for transfers between devices, body(): from_left = lax.ppermute(w_part_full, 'dp', up_x)  44.4 us
    ppermute x1, waiting for transfers between devices, body(): far_a = lax.ppermute(from_left[:, :half_part], 'dp', up_x)  16 us
    unnamed x34, local copies, waits for them, and re-layouts  14.8 us
    dot_general x1, matrix products, body(): out_own = jnp.dot(tokens, w_own, preferred_element_type=f32)  11.5 us
    all_to_all x1, waiting for transfers between devices, body(): got = lax.all_to_all(send, 'dp', split_axis=0, concat_axis=0, tiled=True)  10.9 us
    dot_general x1, matrix products, body(): out_partner = jnp.dot(tokens, w_partner, preferred_element_type=f32)  9.59 us
    dot_general x1, matrix products, body(): lax.dot_general(masked_back, tokens, contract, preferred_element_type=f32)  9.36 us
  transfers between devices with their start and end apart: 10, of which 7 were waited for; matrix products, arithmetic and copies ran while one was open for 29% of the time, Pallas kernels for 0%

commit v1 on v0

--- a/solution.py
+++ b/solution.py
@@ -34,7 +34,14 @@
     w_part = lax.dynamic_slice_in_dim(
         frozen_value_matrix, group_index * part_cols, part_cols, axis=1
     )
-    w_part_full = lax.all_gather(w_part, "fsdp", axis=0, tiled=True)
+
+    def _rest_wires(buf):
+        sides = []
+        for _ in range(lax.axis_size("fsdp")):
+            sides.append(buf)
+        return jnp.concatenate(lax.all_to_all(jnp.stack(sides), "fsdp", 0, 0), axis=0)
+
+    w_part_full = _rest_wires(w_part)
     up_x = [(i, (i + 2) % dp_count) for i in range(dp_count)]
     down_x = [(i, (i - 2) % dp_count) for i in range(dp_count)]
     from_left = lax.ppermute(w_part_full, "dp", up_x)

time: 276 us -> 331 us (1.20)
  blocking collectives: 0 us -> 41.2 us
  local copies, waits for them, and re-layouts: 48.5 us -> 71.9 us
  waiting for transfers between devices: 139 us -> 124 us
  starting transfers between devices: 20 us -> 23.7 us
    all_to_all x0 -> x1, blocking collectives: none -> 41.2 us  [_rest_wires(): lax.all_to_all(jnp.stack(sides), 'fsdp', 0, 0)]
    concatenate x1, local copies, waits for them, and re-layouts: 1.46 us -> 14.4 us  [body(): w_own = jnp.concatenate(same_parity, axis=1)]
    all_gather x1 -> x0, waiting for transfers between devices: 9.21 us -> none  [body(): w_part_full = lax.all_gather(w_part, 'fsdp', axis=0, tiled=True)]
    unnamed x34 -> x33, local copies, waits for them, and re-layouts: 14.8 us -> 8.6 us
    slice x1 -> x2, local copies, waits for them, and re-layouts: 0.07 us -> 6.29 us  [body(): far_b = lax.ppermute(from_right[:, half_part:], 'dp', down_x)]
    ppermute x1, waiting for transfers between devices: 16 us -> 11 us  [body(): far_a = lax.ppermute(from_left[:, :half_part], 'dp', up_x)]
    ppermute x0 -> x2, local copies, waits for them, and re-layouts: none -> 4.59 us  [the longest x1 2.72 us: body(): far_b = lax.ppermute(from_right[:, half_part:], 'dp', down_x)]
    ppermute x1, waiting for transfers between devices: 44.4 us -> 40.5 us  [body(): from_left = lax.ppermute(w_part_full, 'dp', up_x)]
  transfers between devices with their start and end apart: 10 -> 9, of which waited for: 7 -> 6; matrix products, arithmetic and copies ran while one was open for 29% -> 19% of each run, Pallas kernels for 0% -> 0%
where the time goes in v1:
time: 331 us; the launch traced here: 330 us
  waiting for transfers between devices  124 us (37%)
  local copies, waits for them, and re-layouts  71.9 us (22%)
  blocking collectives  41.2 us (12%)
  matrix products  36.2 us (11%)
  starting transfers between devices  23.7 us (7%)
  other arithmetic  18.7 us (6%)
  between operations  14.5 us (4%)
    all_gather x1, waiting for transfers between devices, body(): shares = lax.all_gather(slab, 'fsdp', axis=0, tiled=False)  56.5 us
    all_to_all x1, blocking collectives, _rest_wires(): lax.all_to_all(jnp.stack(sides), 'fsdp', 0, 0)  41.2 us
    ppermute x1, waiting for transfers between devices, body(): from_left = lax.ppermute(w_part_full, 'dp', up_x)  40.5 us
    concatenate x1, local copies, waits for them, and re-layouts, body(): w_own = jnp.concatenate(same_parity, axis=1)  14.4 us
    dot_general x1, matrix products, body(): out_own = jnp.dot(tokens, w_own, preferred_element_type=f32)  11.3 us
    ppermute x1, waiting for transfers between devices, body(): far_a = lax.ppermute(from_left[:, :half_part], 'dp', up_x)  11 us
    all_to_all x1, waiting for transfers between devices, body(): got = lax.all_to_all(send, 'dp', split_axis=0, concat_axis=0, tiled=True)  10.9 us
    dot_general x1, matrix products, body(): out_partner = jnp.dot(tokens, w_partner, preferred_element_type=f32)  9.61 us
  transfers between devices with their start and end apart: 9, of which 6 were waited for; matrix products, arithmetic and copies ran while one was open for 19% of the time, Pallas kernels for 0%

profile of v1, /device:TPU:1, one launch (start us, length us, event | category | flops | bytes accessed | tf_op | source)
XLA Modules:
  0.0 329.8 jit_solution(3641484779301759075)
XLA Ops:
  11.2 2.8 gather_fusion.2
  15.2 5.8 %all-to-all-start.1 = ((bf16[8,64,576]{2,1,0:T(8,128)(2,1)}), bf16[8,64,576]{2,1,0:T(8,128)(2,1)S(1)}, u32[]{:S(2)}, u32[]{:S(2)}) async-start(bf16[8,64,576]{2,1,0:T(8,128)(2,1)} %maximum_select_fusion), calls=%async_computation.1 | async-start | bytes 1310720 | tf_op jit(solution)/shard_map/all_to_all | solution.py:82
  21.1 10.9 %all-to-all-done.1 = bf16[8,64,576]{2,1,0:T(8,128)(2,1)S(1)} async-done(((bf16[8,64,576]{2,1,0:T(8,128)(2,1)}), bf16[8,64,576]{2,1,0:T(8,128)(2,1)S(1)}, u32[]{:S(2)}, u32[]{:S(2)}) %all-to-all-start.1) | async-done | bytes 589856 | tf_op jit(solution)/shard_map/all_to_all | solution.py:82
  34.3 56.5 %all-gather.2.cloned.1.call-done = bf16[16,4,64,576]{3,2,1,0:T(8,128)(2,1)} async-done(((bf16[1,4,64,576]{3,2,1,0:T(8,128)(2,1)}), bf16[16,4,64,576]{3,2,1,0:T(8,128)(2,1)}) %all-gather.2.cloned.1.call-update) | async-done | bytes 4718608 | tf_op jit(solution)/shard_map/all_gather | solution.py:85
  102.9 4.4 %copy.70 = bf16[32,8,16,512]{3,1,2,0:T(8,128)(2,1)S(1)} copy(bf16[32,8,16,512]{3,2,1,0:T(8,128)(2,1)S(1)} %bitcast.103) | data formatting | bytes 8388608
  115.2 9.1 %fusion.22 = f32[256,8192]{1,0:T(8,128)} fusion(bf16[512,256]{0,1:T(8,128)(2,1)S(1)} %bitcast.118, bf16[512,8192]{1,0:T(8,128)(2,1)} %param.8), kind=kOutput, calls=%fused_computation.122 | convolution fusion | flops 2147483648 | bytes 17039360 | tf_op jit(solution)/shard_map/dot_general | solution.py:112
  124.4 8.0 %pad_maximum_fusion = f32[288,8192]{1,0:T(8,128)} fusion(f32[32,8192]{1,0:T(8,128)S(1)} %bitcast.113, f32[256,8192]{1,0:T(8,128)} %fusion.22), kind=kLoop, calls=%fused_computation.8 | loop fusion | flops 2359296 | bytes 18874368 | tf_op jit(solution)/shard_map/concatenate | solution.py:125
  132.8 41.2 %all_to_all.15 = bf16[16,512,128]{1,2,0:T(8,128)(2,1)} all-to-all(bf16[16,512,128]{1,2,0:T(8,128)(2,1)S(1)} %stack.2), channel_id=1, replica_groups=mesh['dp'=8,'fsdp'=16] {'fsdp'}, dimensions={0} | all-to-all | bytes 4194304 | tf_op jit(solution)/shard_map/all_to_all | solution.py:42
  174.0 3.1 copy.50
  179.8 40.5 %collective-permute-done = bf16[8192,128]{1,0:T(8,128)(2,1)S(1)} collective-permute-done((bf16[8192,128]{1,0:T(8,128)(2,1)S(1)}, bf16[8192,128]{1,0:T(8,128)(2,1)S(1)}, u32[]{:S(2)}, u32[]{:S(2)}) %collective-permute-start) | collective-permute-done | bytes 2097184 | tf_op jit(solution)/shard_map/ppermute | solution.py:47
  221.6 2.7 copy.51
  224.3 3.6 %slice.45 = bf16[8192,64]{1,0:T(8,128)(2,1)} slice(bf16[8192,128]{1,0:T(8,128)(2,1)} %collective-permute-done.2), slice={[0:8192], [64:128]} | slice | bytes 2097152 | tf_op jit(solution)/shard_map/slice | solution.py:51
  227.9 2.7 copy.52
  230.6 2.7 collective-permute-start.3
  233.2 11.0 %collective-permute-done.1 = bf16[8192,64]{0,1:T(8,128)(2,1)S(1)} collective-permute-done((bf16[8192,64]{0,1:T(8,128)(2,1)}, bf16[8192,64]{0,1:T(8,128)(2,1)S(1)}, u32[]{:S(2)}, u32[]{:S(2)}) %collective-permute-start.1) | collective-permute-done | bytes 1048608 | tf_op jit(solution)/shard_map/ppermute | solution.py:50
  246.1 3.5 %collective-permute-done.3 = bf16[8192,64]{0,1:T(8,128)(2,1)} collective-permute-done((bf16[8192,64]{0,1:T(8,128)(2,1)}, bf16[8192,64]{0,1:T(8,128)(2,1)}, u32[]{:S(2)}, u32[]{:S(2)}) %collective-permute-start.3) | collective-permute-done | bytes 1048608 | tf_op jit(solution)/shard_map/ppermute | solution.py:51
  249.6 2.7 copy.54
  252.3 14.4 %concatenate.15 = bf16[8192,512]{1,0:T(8,128)(2,1)} concatenate(bf16[8192,128]{1,0:T(8,128)(2,1)S(1)} %bitcast.107, bf16[8192,128]{1,0:T(8,128)(2,1)} %copy-done.3, bf16[8192,64]{1,0:T(8,128)(2,1)} %copy.53, bf16[8192,64]{1,0:T(8,128)(2,1)} %copy.54, bf16[8192,128]{1,0:T(8,128)(2,1)} %collective-permute-done.2), dimensions={1} | concatenate | bytes 16777216 | tf_op jit(solution)/shard_map/concatenate | solution.py:54
  266.7 7.3 %collective-permute-start.4 = (bf16[8192,512]{1,0:T(8,128)(2,1)}, bf16[8192,512]{1,0:T(8,128)(2,1)}, u32[]{:S(2)}, u32[]{:S(2)}) collective-permute-start(bf16[8192,512]{1,0:T(8,128)(2,1)} %concatenate.15), channel_id=1, source_target_pairs={{0,16},{16,0},{32,48},{48,32},{64,80},{80,64},{96,112},{112,96},{1... | collective-permute-start | bytes 25165832 | tf_op jit(solution)/shard_map/ppermute | solution.py:55
  274.3 11.3 %convolution_bitcast_fusion.2 = f32[512,512]{0,1:T(8,128)} fusion(bf16[8192,512]{1,0:T(8,128)(2,1)} %concatenate.15, bf16[512,8192]{1,0:T(8,128)(2,1)} %param.8), kind=kOutput, calls=%fused_computation.14 | convolution fusion | flops 4294967296 | bytes 17825792 | tf_op jit(solution)/shard_map/dot_general | solution.py:56
  289.5 5.1 %all-to-all-start.2 = ((f32[8,72,512]{2,1,0:T(8,128)}), f32[8,72,512]{2,1,0:T(8,128)}, u32[]{:S(2)}, u32[]{:S(2)}) async-start(f32[8,72,512]{2,1,0:T(8,128)} %select_select_fusion), calls=%async_computation.3 | async-start | bytes 2359296 | tf_op jit(solution)/shard_map/all_to_all | solution.py:140
  294.5 9.6 %convolution_bitcast_fusion.1 = f32[512,512]{0,1:T(8,128)S(1)} fusion(bf16[8192,512]{1,0:T(8,128)(2,1)} %collective-permute-done.4, bf16[512,8192]{1,0:T(8,128)(2,1)} %param.8), kind=kOutput, calls=%fused_computation.13 | convolution fusion | flops 4294967296 | bytes 17825792 | tf_op jit(solution)/shard_map/dot_general | solution.py:57
  312.8 4.5 %broadcast_in_dim.151 = f32[64,64,512]{2,1,0:T(8,128)} broadcast(f32[]{:T(128)} %constant.200.clone.1), dimensions={} | broadcast | bytes 8388612 | tf_op jit(solution)/shard_map/broadcast_in_dim | solution.py:143
  317.3 3.2 scatter_fusion
  (106 shorter events, 49.0 us)
Async XLA Ops:
  7.2 125.2 %copy-start = (bf16[512,1024]{1,0:T(8,128)(2,1)S(1)}, bf16[512,1024]{1,0:T(8,128)(2,1)}, u32[]{:S(2)}) copy-start(bf16[512,1024]{1,0:T(8,128)(2,1)} %param.9) | copy-start | bytes 3145732
  7.2 1.0 copy-start.2
  14.2 19.3 %copy-start.10 = (s32[1,64]{1,0:T(1,128)S(1)}, s32[1,64]{1,0:T(1,128)}, u32[]{:S(2)}) copy-start(s32[1,64]{1,0:T(1,128)} %param.13) | copy-start | bytes 772
  14.2 19.5 %copy-start.6 = (bf16[512,1024]{1,0:T(8,128)(2,1)S(1)}, bf16[512,1024]{1,0:T(8,128)(2,1)}, u32[]{:S(2)}) copy-start(bf16[512,1024]{1,0:T(8,128)(2,1)} %param.12) | copy-start | bytes 3145732
  15.2 16.7 %all-to-all-start.1 = ((bf16[8,64,576]{2,1,0:T(8,128)(2,1)}), bf16[8,64,576]{2,1,0:T(8,128)(2,1)S(1)}, u32[]{:S(2)}, u32[]{:S(2)}) async-start(bf16[8,64,576]{2,1,0:T(8,128)(2,1)} %maximum_select_fusion), calls=%async_computation.1 | async-start | bytes 1310720 | tf_op jit(solution)/shard_map/all_to_all | solution.py:82
  21.0 69.7 %all-gather.2.cloned.1.call-start = ((), (), s32[]{:S(2)}) async-start(), calls=%async_computation.4 | async-start | bytes 5570560 | tf_op jit(solution)/shard_map/all_gather | solution.py:85
  33.4 252.2 %reduce-scatter.2.cloned.1.call-start = ((), (), s32[]{:S(2)}) async-start(), calls=%async_computation.5 | async-start | bytes 10027008 | tf_op jit(solution)/shard_map/reduce_scatter | solution.py:126
  95.9 4.6 %copy-start.4 = (bf16[256,1024]{1,0:T(8,128)(2,1)}, bf16[256,1024]{1,0:T(8,128)(2,1)S(1)}, u32[]{:S(2)}) copy-start(bf16[256,1024]{1,0:T(8,128)(2,1)S(1)} %reshape_reshape.7) | copy-start | bytes 1572868
  100.5 6.8 %slice-start = ((s8[8388608]{0:T(1024)(128)(4,1)}), s8[4194304]{0:T(1024)(128)(4,1)S(1)}, s32[]{:S(2)}) async-start(s8[8388608]{0:T(1024)(128)(4,1)} %bitcast.109), calls=%async_computation.6 | async-start | bytes 8388608
  102.9 4.4 %slice-start.1 = ((s8[8388608]{0:T(1024)(128)(4,1)}), s8[4194304]{0:T(1024)(128)(4,1)S(1)}, s32[]{:S(2)}) async-start(s8[8388608]{0:T(1024)(128)(4,1)} %bitcast.109), calls=%async_computation.7 | async-start | bytes 8388608
  177.0 43.2 %collective-permute-start = (bf16[8192,128]{1,0:T(8,128)(2,1)S(1)}, bf16[8192,128]{1,0:T(8,128)(2,1)S(1)}, u32[]{:S(2)}, u32[]{:S(2)}) collective-permute-start(bf16[8192,128]{1,0:T(8,128)(2,1)S(1)} %bitcast.105), channel_id=1, source_target_pairs={{0,32},{16,48},{32,64},{48,80},{64,96},{80,112},{96,0},{112,16},{1... | collective-permute-start | bytes 6291464 | tf_op jit(solution)/shard_map/ppermute | solution.py:47
  178.3 46.0 %collective-permute-start.2 = (bf16[8192,128]{1,0:T(8,128)(2,1)S(1)}, bf16[8192,128]{1,0:T(8,128)(2,1)}, u32[]{:S(2)}, u32[]{:S(2)}) collective-permute-start(bf16[8192,128]{1,0:T(8,128)(2,1)S(1)} %bitcast.106), channel_id=1, source_target_pairs={{0,96},{16,112},{32,0},{48,16},{64,32},{80,48},{96,64},{112,80},{1... | collective-permute-start | bytes 6291464 | tf_op jit(solution)/shard_map/ppermute | solution.py:48
  220.3 1.3 copy-start.3
  224.3 20.0 %collective-permute-start.1 = (bf16[8192,64]{0,1:T(8,128)(2,1)}, bf16[8192,64]{0,1:T(8,128)(2,1)S(1)}, u32[]{:S(2)}, u32[]{:S(2)}) collective-permute-start(bf16[8192,64]{0,1:T(8,128)(2,1)} %copy.51), channel_id=1, source_target_pairs={{0,32},{16,48},{32,64},{48,80},{64,96},{80,112},{96,0},{112,16},{1... | collective-permute-start | bytes 3145736 | tf_op jit(solution)/shard_map/ppermute | solution.py:50
  230.6 19.0 %collective-permute-start.3 = (bf16[8192,64]{0,1:T(8,128)(2,1)}, bf16[8192,64]{0,1:T(8,128)(2,1)}, u32[]{:S(2)}, u32[]{:S(2)}) collective-permute-start(bf16[8192,64]{0,1:T(8,128)(2,1)} %copy.52), channel_id=1, source_target_pairs={{0,96},{16,112},{32,0},{48,16},{64,32},{80,48},{96,64},{112,80},{1... | collective-permute-start | bytes 3145736 | tf_op jit(solution)/shard_map/ppermute | solution.py:51
  266.7 27.8 %collective-permute-start.4 = (bf16[8192,512]{1,0:T(8,128)(2,1)}, bf16[8192,512]{1,0:T(8,128)(2,1)}, u32[]{:S(2)}, u32[]{:S(2)}) collective-permute-start(bf16[8192,512]{1,0:T(8,128)(2,1)} %concatenate.15), channel_id=1, source_target_pairs={{0,16},{16,0},{32,48},{48,32},{64,80},{80,64},{96,112},{112,96},{1... | collective-permute-start | bytes 25165832 | tf_op jit(solution)/shard_map/ppermute | solution.py:55
  289.5 21.7 %all-to-all-start.2 = ((f32[8,72,512]{2,1,0:T(8,128)}), f32[8,72,512]{2,1,0:T(8,128)}, u32[]{:S(2)}, u32[]{:S(2)}) async-start(f32[8,72,512]{2,1,0:T(8,128)} %select_select_fusion), calls=%async_computation.3 | async-start | bytes 2359296 | tf_op jit(solution)/shard_map/all_to_all | solution.py:140
  294.5 9.6 %copy-start.9 = (f32[512,512]{0,1:T(8,128)S(1)}, f32[512,512]{0,1:T(8,128)}, u32[]{:S(2)}) copy-start(f32[512,512]{0,1:T(8,128)} %convolution_bitcast_fusion.2) | copy-start | bytes 3145732
  306.3 2.0 copy-start.5
  306.4 2.0 copy-start.8
  317.3 5.7 %copy-start.1 = (bf16[512,1024]{1,0:T(8,128)(2,1)S(1)}, bf16[512,1024]{1,0:T(8,128)(2,1)}, u32[]{:S(2)}) copy-start(bf16[512,1024]{1,0:T(8,128)(2,1)} %param.9) | copy-start | bytes 3145732
  321.7 1.3 copy-start.7
Sparse Core Ops, SparseCore 0:
  33.5 57.1 all-gather.1
  132.5 101.0 reduce-scatter.1
